TPU v7x, 256 devices: a whole 4x4x8 slice. The times are simulated.
256 devices in a mesh: px: 32 (over z, x_hi, core), py: 8 (over y, x_lo).
Axes of the slice: x: 4 (x_hi: 2, x_lo: 2; x = x_hi * 2 + x_lo), y: 4, z: 8, core: 2. Of those that a mesh axis runs over, the one named last changes fastest.
Arguments:
- table: float32 [25, 50, 1000], replicated, may hold values from -1 to 1
- charge: float32 [128, 32, 8], P('px', 'py'), may hold values from 0.1 to 1
- hit_bins: int32 [128, 32, 8], P('px', 'py'), may hold values from 0 to 49
- hit_ticks: int32 [128, 32, 8], P('px', 'py'), may hold values from 0 to 23
- active: int32 [128, 32], P('px', 'py'), may hold values 0 or 1
- measured: bfloat16 [128, 32, 1024], P('px', 'py'), may hold values from -6 to 6
- row_module: int32 [128], replicated, may hold values from 0 to 6, as said below
- col_module: int32 [32], replicated, may hold values from 0 to 4, as said below
Outputs:
- current: bfloat16 [128, 32, 1024], P('px', 'py')
- table_grad: float32 [25, 50, 1000], P(None, None, 'py')
Inputs may be any that keep to these rules, and one draw needn't show every extreme that they name: `row_module`: starts at 0 and never falls; it rises by one at 6 rows. `col_module`: starts at 0 and never falls; it rises by one at 4 columns.
All inputs are finite; a program needn't handle non-finite values. No bound on the sum of `active` on one device may be relied on, other than what follows from the above.
Results may differ from a plain program's by a relative error of at most 0.014.
Values may be sent and summed in bfloat16 or wider, within the bound.
No kernel may reach another device: no remote copies, remote signals or barrier semaphores. Data moves between devices by JAX's collectives and lax.ppermute only.
A program may use at most 128 MiB of HBM per device.

v0:
```python
import jax
import jax.numpy as jnp
from jax import lax
from jax.sharding import PartitionSpec as P

BINS = 50
SHIFTS = 24


def passed_along(block, axis, distance):
    devices = range(lax.axis_size(axis))
    route = [(i - distance, i) for i in devices if i - distance in devices]
    return lax.ppermute(block, axis, route)


def bin_charges(charge, hit_bins, hit_ticks):
    tick_hot = (hit_ticks[..., None] == jnp.arange(SHIFTS, dtype=jnp.int32)).astype(jnp.float32)
    bin_hot = (hit_bins[..., None] == jnp.arange(BINS, dtype=jnp.int32)).astype(jnp.float32)
    weighted = charge[..., None] * tick_hot
    return jnp.einsum("xyks,xykb->xysb", weighted, bin_hot).astype(jnp.bfloat16)


def gather_offsets(source, rows, cols, count_x, count_y):
    pieces = []
    for row_off in range(-2, 3):
        for col_off in range(-2, 3):
            partial_value = source[
                2 - row_off : 2 - row_off + count_x, 2 - col_off : 2 - col_off + count_y
            ]
            row_same = rows[2 - row_off : 2 - row_off + count_x] == rows[2 : 2 + count_x]
            col_same = cols[2 - col_off : 2 - col_off + count_y] == cols[2 : 2 + count_y]
            allowed = row_same[:, None] & col_same[None, :]
            pieces.append(
                jnp.where(
                    allowed[:, :, None, None], partial_value, jnp.zeros((), partial_value.dtype)
                )
            )
    return jnp.stack(pieces, 0)


def shift_sum(partial_value, ticks):
    total = jnp.zeros(partial_value.shape[:2] + (ticks + SHIFTS,), jnp.float32)
    for offset in range(SHIFTS):
        total = total + jnp.pad(
            partial_value[:, :, offset, :], ((0, 0), (0, 0), (offset, SHIFTS - offset))
        )
    return total


def windows(resid, ticks):
    return jnp.stack([resid[:, :, offset : offset + ticks] for offset in range(SHIFTS)], axis=2)


def residual_of(prediction, measured, active):
    return (
        (prediction - measured.astype(jnp.float32)) * active.astype(jnp.float32)[..., None]
    ).astype(jnp.bfloat16)


def on_device(table, charge, hit_bins, hit_ticks, active, measured, row_module, col_module):
    tile_x, tile_y = (charge.shape[0], charge.shape[1])
    ticks = table.shape[2]
    parts_y = lax.axis_size("py")
    share = ticks // parts_y
    span = share + SHIFTS - 1
    weights = table.astype(jnp.bfloat16)
    row_start = lax.axis_index("px") * tile_x
    col_start = lax.axis_index("py") * tile_y
    deposits = jnp.stack(
        [charge, hit_bins.astype(jnp.float32), hit_ticks.astype(jnp.float32)], axis=-1
    )
    band = lax.all_gather(deposits, "py", axis=1, tiled=True)
    above = passed_along(band[tile_x - 2 :], "px", 1)
    below = passed_along(band[:2], "px", -1)
    wide = jnp.concatenate([above, band, below], axis=0)
    binned = bin_charges(
        wide[..., 0], wide[..., 1].astype(jnp.int32), wide[..., 2].astype(jnp.int32)
    )
    source = jnp.pad(binned, ((0, 0), (2, 2), (0, 0), (0, 0)))
    width = source.shape[1] - 4
    rows_wide = lax.dynamic_slice_in_dim(
        jnp.pad(row_module, 2, constant_values=-1), row_start, tile_x + 4, 0
    )
    cols_all = jnp.pad(col_module, 2, constant_values=-1)
    own_source = lax.dynamic_slice_in_dim(source, col_start, tile_y + 4, 1)
    own_cols = lax.dynamic_slice_in_dim(cols_all, col_start, tile_y + 4, 0)
    stacked = gather_offsets(own_source, rows_wide, own_cols, tile_x, tile_y)
    partial_value = jnp.einsum(
        "oxysb,obt->xyst", stacked, weights, preferred_element_type=jnp.float32
    )
    prediction = shift_sum(partial_value, ticks)
    resid = residual_of(prediction, measured, active)
    sent = jnp.stack([resid[:, :, k * share : k * share + span] for k in range(parts_y)], axis=0)
    got = lax.all_to_all(sent, "py", 0, 0)
    band_resid = jnp.transpose(got, (1, 0, 2, 3)).reshape(tile_x, width, span)
    stacked_band = gather_offsets(source, rows_wide, cols_all, tile_x, width)
    gradient = jnp.einsum(
        "oxysb,xysu->obu",
        stacked_band,
        windows(band_resid, share),
        preferred_element_type=jnp.float32,
    )
    summed = lax.psum(gradient, "px")
    return (prediction.astype(jnp.bfloat16), summed / 16)


def solution(mesh):
    in_specs = (
        P(),
        P("px", "py", None),
        P("px", "py", None),
        P("px", "py", None),
        P("px", "py"),
        P("px", "py", None),
        P(),
        P(),
    )
    out_specs = (P("px", "py", None), P(None, None, "py"))
    return jax.shard_map(
        on_device, mesh=mesh, in_specs=in_specs, out_specs=out_specs, check_vma=False
    )
```

profile of v0, /device:TPU:101, one launch (start us, length us, event | category | flops | bytes accessed | tf_op | source)
XLA Modules:
  0.0 386.6 jit_solution(15461394324954869272)
XLA Ops:
  7.2 0.7 convert_bitcast_fusion
  7.9 0.7 pad_maximum_fusion.1
  8.6 22.5 %all_gather.3 = f32[4,32,8,3]{2,0,3,1:T(4,128)S(1)} all-gather(f32[4,4,8,3]{2,0,3,1:T(4,128)S(1)} %copy.144), channel_id=1, replica_groups=mesh['px'=32,'py'=8] {'py'}, dimensions={1}, use_global_device_ids=true | all-gather | bytes 13824 | tf_op jit(solution)/shard_map/all_gather | solution.py:72
  31.2 8.9 %collective-permute-start.1 = (f32[2,32,8,3]{2,0,3,1:T(2,128)S(1)}, f32[2,32,8,3]{2,0,3,1:T(2,128)S(1)}, u32[]{:S(2)}, u32[]{:S(2)}) collective-permute-start(f32[2,32,8,3]{2,0,3,1:T(2,128)S(1)} %get-tuple-element.30), channel_id=1, source_target_pairs={{8,0},{16,8},{24,16},{32,24},{40,32},{48,40},{56,48},{64,56},{72,6... | collective-permute-start | bytes 18440 | tf_op jit(solution)/shard_map/ppermute | solution.py:13
  40.1 4.6 %collective-permute-start = (f32[2,32,8,3]{2,0,3,1:T(2,128)S(1)}, f32[2,32,8,3]{2,0,3,1:T(2,128)S(1)}, u32[]{:S(2)}, u32[]{:S(2)}) collective-permute-start(f32[2,32,8,3]{2,0,3,1:T(2,128)S(1)} %get-tuple-element.29), channel_id=1, source_target_pairs={{0,8},{8,16},{16,24},{24,32},{32,40},{40,48},{48,56},{56,64},{64,7... | collective-permute-start | bytes 18440 | tf_op jit(solution)/shard_map/ppermute | solution.py:13
  44.7 0.9 slice_compare_fusion
  45.6 0.7 pad_dynamic-slice_fusion.1
  46.4 0.7 pad_dynamic-slice_fusion
  47.4 0.7 convert_element_type.92
  48.7 2.9 convolution_convert_fusion
  54.3 1.3 slice-done
  56.1 2.6 fusion
  59.2 1.2 fusion.46
  69.5 2.0 multiply_convert_fusion
  71.5 4.6 %copy-done.1 = bf16[25,4,32,24,50]{4,3,2,1,0:T(8,128)(2,1)} copy-done((bf16[25,4,32,24,50]{4,3,2,1,0:T(8,128)(2,1)}, bf16[25,4,32,24,50]{4,3,2,1,0:T(8,128)(2,1)S(1)}, u32[]{:S(2)}) %copy-start.1) | copy-done | bytes 7680024
  76.7 0.7 constant_dynamic-update-slice_fusion.31
  81.4 5.4 %all-to-all-start = ((bf16[8,4,4,148]{3,2,1,0:T(4,128)(2,1)}), bf16[8,4,4,148]{3,2,1,0:T(4,128)(2,1)S(1)}, u32[]{:S(2)}, u32[]{:S(2)}) async-start(bf16[8,4,4,148]{3,2,1,0:T(4,128)(2,1)} %constant_dynamic-update-slice_fusion.25), calls=%async_computation | async-start | bytes 131072 | tf_op jit(solution)/shard_map/all_to_all | solution.py:94
  86.8 1.1 bitcast_dynamic-update-slice_fusion.1
  88.0 1.1 bitcast_dynamic-update-slice_fusion
  89.1 2.9 all-to-all-done
  94.0 2.6 stack.359
  96.6 12.7 %convolution_bitcast_fusion = f32[25,50,125]{2,1,0:T(8,128)} fusion(bf16[25,4,32,24,50]{4,3,2,1,0:T(8,128)(2,1)} %bitcast_dynamic-update-slice_fusion, bf16[4,32,24,125]{3,2,1,0:T(8,128)(2,1)S(1)} %stack.359), kind=kOutput, calls=%fused_computation.6 | convolution fusion | flops 960000000 | bytes 9073000 | tf_op jit(solution)/shard_map/oxysb,xysu->obu/dot_general | solution.py:97
  109.3 268.5 %all-reduce.29.cloned.1.call-done = f32[25,50,125]{2,1,0:T(8,128)} async-done(((f32[25,50,125]{2,1,0:T(8,128)}), f32[25,50,125]{2,1,0:T(8,128)}) %all-reduce.29.cloned.1.call-update) | async-done | bytes 625016 | tf_op jit(solution)/shard_map/psum | solution.py:103
  377.8 2.0 broadcast_multiply_fusion
  (134 shorter events, 19.8 us)
Async XLA Ops:
  31.2 16.9 %collective-permute-start.1 = (f32[2,32,8,3]{2,0,3,1:T(2,128)S(1)}, f32[2,32,8,3]{2,0,3,1:T(2,128)S(1)}, u32[]{:S(2)}, u32[]{:S(2)}) collective-permute-start(f32[2,32,8,3]{2,0,3,1:T(2,128)S(1)} %get-tuple-element.30), channel_id=1, source_target_pairs={{8,0},{16,8},{24,16},{32,24},{40,32},{48,40},{56,48},{64,56},{72,6... | collective-permute-start | bytes 18440 | tf_op jit(solution)/shard_map/ppermute | solution.py:13
  40.1 8.2 %collective-permute-start = (f32[2,32,8,3]{2,0,3,1:T(2,128)S(1)}, f32[2,32,8,3]{2,0,3,1:T(2,128)S(1)}, u32[]{:S(2)}, u32[]{:S(2)}) collective-permute-start(f32[2,32,8,3]{2,0,3,1:T(2,128)S(1)} %get-tuple-element.29), channel_id=1, source_target_pairs={{0,8},{8,16},{16,24},{24,32},{32,40},{40,48},{48,56},{56,64},{64,7... | collective-permute-start | bytes 18440 | tf_op jit(solution)/shard_map/ppermute | solution.py:13
  53.4 2.2 slice-start
  53.7 2.4 slice-start.1
  68.7 0.8 copy-start
  69.4 6.7 %copy-start.1 = (bf16[25,4,32,24,50]{4,3,2,1,0:T(8,128)(2,1)}, bf16[25,4,32,24,50]{4,3,2,1,0:T(8,128)(2,1)S(1)}, u32[]{:S(2)}) copy-start(bf16[25,4,32,24,50]{4,3,2,1,0:T(8,128)(2,1)S(1)} %fusion.6) | copy-start | bytes 23040004
  81.4 10.6 %all-to-all-start = ((bf16[8,4,4,148]{3,2,1,0:T(4,128)(2,1)}), bf16[8,4,4,148]{3,2,1,0:T(4,128)(2,1)S(1)}, u32[]{:S(2)}, u32[]{:S(2)}) async-start(bf16[8,4,4,148]{3,2,1,0:T(4,128)(2,1)} %constant_dynamic-update-slice_fusion.25), calls=%async_computation | async-start | bytes 131072 | tf_op jit(solution)/shard_map/all_to_all | solution.py:94
  86.8 291.0 %all-reduce.29.cloned.1.call-start = ((), (), s32[]{:S(2)}) async-start(), calls=%async_computation.1 | async-start | bytes 1433600 | tf_op jit(solution)/shard_map/psum | solution.py:103
Sparse Core Ops, SparseCore 0:
  109.4 268.2 all-reduce.28
where the time goes:
time: 387 us
  waiting for transfers between devices  271 us (70%)
  blocking collectives  22.5 us (6%)
  local copies, waits for them, and re-layouts  21.4 us (6%)
  other arithmetic  19.5 us (5%)
  starting transfers between devices  18.9 us (5%)
  matrix products  18.2 us (5%)
  between operations  14.8 us (4%)
    psum x1, waiting for transfers between devices, on_device(): summed = lax.psum(gradient, 'px')  268 us
    all_gather x1, blocking collectives, on_device(): band = lax.all_gather(deposits, 'py', axis=1, tiled=True)  22.5 us
    ppermute x2, starting transfers between devices, passed_along(): return lax.ppermute(block, axis, route)  13.4 us
    dot_general x1, matrix products, on_device(): jnp.einsum('oxysb,xysu->obu', stacked_band, windows(band_resid, share), p...  12.7 us
    unnamed x41, local copies, waits for them, and re-layouts  12.4 us
    unnamed x47, other arithmetic  10.9 us
  transfers between devices with their start and end apart: 4, of which 2 were waited for; matrix products, arithmetic and copies ran while one was open for 2% of the time, Pallas kernels for 0%

commit v1 on v0

--- a/solution.py
+++ b/solution.py
@@ -100,7 +100,12 @@
         windows(band_resid, share),
         preferred_element_type=jnp.float32,
     )
-    summed = lax.psum(gradient, "px")
+
+    def get_the_flows(local_values, across):
+        opened = lax.all_gather(local_values, across).sum(axis=0)
+        return opened
+
+    summed = get_the_flows(gradient, "px")
     return (prediction.astype(jnp.bfloat16), summed / 16)
 
 

time: 387 us -> 296 us (0.76); the launches traced: 387 us -> 291 us
  waiting for transfers between devices: 271 us -> 168 us
  other arithmetic: 19.5 us -> 26.9 us
    psum x1 -> x0, waiting for transfers between devices: 268 us -> none  [on_device(): summed = lax.psum(gradient, 'px')]
    all_gather x0 -> x1, waiting for transfers between devices: none -> 165 us  [get_the_flows(): opened = lax.all_gather(local_values, across).sum(axis=0)]
    reduce_sum x0 -> x1, other arithmetic: none -> 8.52 us  [get_the_flows(): opened = lax.all_gather(local_values, across).sum(axis=0)]
where the time goes in v1:
time: 296 us; the launch traced here: 291 us
  waiting for transfers between devices  168 us (57%)
  other arithmetic  26.9 us (9%)
  blocking collectives  22.5 us (8%)
  local copies, waits for them, and re-layouts  21.4 us (7%)
  starting transfers between devices  18.9 us (6%)
  matrix products  18.2 us (6%)
  between operations  14.8 us (5%)
    all_gather x1, waiting for transfers between devices, get_the_flows(): opened = lax.all_gather(local_values, across).sum(axis=0)  165 us
    all_gather x1, blocking collectives, on_device(): band = lax.all_gather(deposits, 'py', axis=1, tiled=True)  22.5 us
    ppermute x2, starting transfers between devices, passed_along(): return lax.ppermute(block, axis, route)  13.4 us
    dot_general x1, matrix products, on_device(): jnp.einsum('oxysb,xysu->obu', stacked_band, windows(band_resid, share), p...  12.7 us
    unnamed x41, local copies, waits for them, and re-layouts  12.4 us
    unnamed x47, other arithmetic  10.9 us
    reduce_sum x1, other arithmetic, get_the_flows(): opened = lax.all_gather(local_values, across).sum(axis=0)  8.52 us
  transfers between devices with their start and end apart: 4, of which 2 were waited for; matrix products, arithmetic and copies ran while one was open for 2% of the time, Pallas kernels for 0%

profile of v1, /device:TPU:101, one launch (start us, length us, event | category | flops | bytes accessed | tf_op | source)
XLA Modules:
  0.0 290.8 jit_solution(13477713442231197206)
XLA Ops:
  7.2 0.7 convert_bitcast_fusion
  7.9 0.7 pad_maximum_fusion.1
  8.6 22.5 %all_gather.9 = f32[4,32,8,3]{2,0,3,1:T(4,128)S(1)} all-gather(f32[4,4,8,3]{2,0,3,1:T(4,128)S(1)} %copy.144), channel_id=1, replica_groups=mesh['px'=32,'py'=8] {'py'}, dimensions={1}, use_global_device_ids=true | all-gather | bytes 13824 | tf_op jit(solution)/shard_map/all_gather | solution.py:72
  31.2 8.9 %collective-permute-start.1 = (f32[2,32,8,3]{2,0,3,1:T(2,128)S(1)}, f32[2,32,8,3]{2,0,3,1:T(2,128)S(1)}, u32[]{:S(2)}, u32[]{:S(2)}) collective-permute-start(f32[2,32,8,3]{2,0,3,1:T(2,128)S(1)} %get-tuple-element.30), channel_id=1, source_target_pairs={{8,0},{16,8},{24,16},{32,24},{40,32},{48,40},{56,48},{64,56},{72,6... | collective-permute-start | bytes 18440 | tf_op jit(solution)/shard_map/ppermute | solution.py:13
  40.1 4.6 %collective-permute-start = (f32[2,32,8,3]{2,0,3,1:T(2,128)S(1)}, f32[2,32,8,3]{2,0,3,1:T(2,128)S(1)}, u32[]{:S(2)}, u32[]{:S(2)}) collective-permute-start(f32[2,32,8,3]{2,0,3,1:T(2,128)S(1)} %get-tuple-element.29), channel_id=1, source_target_pairs={{0,8},{8,16},{16,24},{24,32},{32,40},{40,48},{48,56},{56,64},{64,7... | collective-permute-start | bytes 18440 | tf_op jit(solution)/shard_map/ppermute | solution.py:13
  44.7 0.9 slice_compare_fusion
  45.6 0.7 pad_dynamic-slice_fusion.1
  46.4 0.7 pad_dynamic-slice_fusion
  47.4 0.7 convert_element_type.92
  48.7 2.9 convolution_convert_fusion
  54.3 1.3 slice-done
  56.1 2.6 fusion
  59.2 1.2 fusion.46
  69.5 2.0 multiply_convert_fusion
  71.5 4.6 %copy-done.1 = bf16[25,4,32,24,50]{4,3,2,1,0:T(8,128)(2,1)} copy-done((bf16[25,4,32,24,50]{4,3,2,1,0:T(8,128)(2,1)}, bf16[25,4,32,24,50]{4,3,2,1,0:T(8,128)(2,1)S(1)}, u32[]{:S(2)}) %copy-start.1) | copy-done | bytes 7680024
  81.4 5.4 %all-to-all-start = ((bf16[8,4,4,148]{3,2,1,0:T(4,128)(2,1)}), bf16[8,4,4,148]{3,2,1,0:T(4,128)(2,1)S(1)}, u32[]{:S(2)}, u32[]{:S(2)}) async-start(bf16[8,4,4,148]{3,2,1,0:T(4,128)(2,1)} %constant_dynamic-update-slice_fusion.25), calls=%async_computation | async-start | bytes 131072 | tf_op jit(solution)/shard_map/all_to_all | solution.py:94
  86.8 1.1 bitcast_dynamic-update-slice_fusion.1
  87.9 1.1 bitcast_dynamic-update-slice_fusion
  89.1 2.9 all-to-all-done
  94.0 2.6 stack.359
  96.6 12.7 %convolution_bitcast_fusion = f32[25,50,125]{2,1,0:T(8,128)} fusion(bf16[25,4,32,24,50]{4,3,2,1,0:T(8,128)(2,1)} %bitcast_dynamic-update-slice_fusion, bf16[4,32,24,125]{3,2,1,0:T(8,128)(2,1)S(1)} %stack.359), kind=kOutput, calls=%fused_computation.6 | convolution fusion | flops 960000000 | bytes 9073000 | tf_op jit(solution)/shard_map/oxysb,xysu->obu/dot_general | solution.py:97
  109.3 165.2 %all-gather.3.cloned.1.call-done = f32[800,50,125]{2,1,0:T(8,128)} async-done(((f32[25,50,125]{2,1,0:T(8,128)}), f32[800,50,125]{2,1,0:T(8,128)}) %all-gather.3.cloned.1.call-update) | async-done | bytes 20000016 | tf_op jit(solution)/shard_map/all_gather | solution.py:105
  274.5 8.5 %reduce_sum.9 = f32[25,50,125]{2,1,0:T(8,128)S(1)} reduce(f32[32,25,50,125]{3,2,1,0:T(8,128)} %bitcast.371, f32[]{:T(128)} %constant.29.clone.1), dimensions={0}, to_apply=%region_0.1 | reduce | flops 4843750 | bytes 20625004 | tf_op jit(solution)/shard_map/reduce_sum | solution.py:105
  283.0 0.9 broadcast_multiply_fusion
  (135 shorter events, 20.5 us)
Async XLA Ops:
  31.2 16.9 %collective-permute-start.1 = (f32[2,32,8,3]{2,0,3,1:T(2,128)S(1)}, f32[2,32,8,3]{2,0,3,1:T(2,128)S(1)}, u32[]{:S(2)}, u32[]{:S(2)}) collective-permute-start(f32[2,32,8,3]{2,0,3,1:T(2,128)S(1)} %get-tuple-element.30), channel_id=1, source_target_pairs={{8,0},{16,8},{24,16},{32,24},{40,32},{48,40},{56,48},{64,56},{72,6... | collective-permute-start | bytes 18440 | tf_op jit(solution)/shard_map/ppermute | solution.py:13
  40.1 8.2 %collective-permute-start = (f32[2,32,8,3]{2,0,3,1:T(2,128)S(1)}, f32[2,32,8,3]{2,0,3,1:T(2,128)S(1)}, u32[]{:S(2)}, u32[]{:S(2)}) collective-permute-start(f32[2,32,8,3]{2,0,3,1:T(2,128)S(1)} %get-tuple-element.29), channel_id=1, source_target_pairs={{0,8},{8,16},{16,24},{24,32},{32,40},{40,48},{48,56},{56,64},{64,7... | collective-permute-start | bytes 18440 | tf_op jit(solution)/shard_map/ppermute | solution.py:13
  53.4 2.2 slice-start
  53.7 2.4 slice-start.1
  68.7 0.8 copy-start
  69.4 6.7 %copy-start.1 = (bf16[25,4,32,24,50]{4,3,2,1,0:T(8,128)(2,1)}, bf16[25,4,32,24,50]{4,3,2,1,0:T(8,128)(2,1)S(1)}, u32[]{:S(2)}) copy-start(bf16[25,4,32,24,50]{4,3,2,1,0:T(8,128)(2,1)S(1)} %fusion.6) | copy-start | bytes 23040004
  81.4 10.6 %all-to-all-start = ((bf16[8,4,4,148]{3,2,1,0:T(4,128)(2,1)}), bf16[8,4,4,148]{3,2,1,0:T(4,128)(2,1)S(1)}, u32[]{:S(2)}, u32[]{:S(2)}) async-start(bf16[8,4,4,148]{3,2,1,0:T(4,128)(2,1)} %constant_dynamic-update-slice_fusion.25), calls=%async_computation | async-start | bytes 131072 | tf_op jit(solution)/shard_map/all_to_all | solution.py:94
  86.8 187.7 %all-gather.3.cloned.1.call-start = ((), (), s32[]{:S(2)}) async-start(), calls=%async_computation.1 | async-start | bytes 23654400 | tf_op jit(solution)/shard_map/all_gather | solution.py:105
Sparse Core Ops, SparseCore 0:
  109.4 165.0 all-gather.2
